TPU v7x, 128 devices: a whole 4x4x4 slice. The times are simulated.
128 devices in a mesh: req: 32 (over z, y, core), seq: 4 (over x).
Axes of the slice: x: 4, y: 4, z: 4, core: 2. Of those that a mesh axis runs over, the one named last changes fastest.
Arguments:
- hidden: bfloat16 [32, 4, 512, 2048], P('req', 'seq'), may hold values from -6 to 6
- w_in: bfloat16 [2048, 4384], P('req', 'seq'), may hold values from -0.125 to 0.125
- conv_weight: float32 [4, 2304], replicated, may hold values from -3 to 3
- conv_bias: float32 [2304], replicated, may hold values from -0.5 to 0.5
- dt_bias: float32 [32], replicated, may hold values from -5 to -2
- a_log: float32 [32], replicated, may hold values from -12 to 2
- d_skip: float32 [32], replicated, may hold values from 0.5 to 1.5
- norm_weight: float32 [2048], replicated, may hold values from 0.5 to 1.5
- lengths: int32 [32], replicated, may hold values from 4 to 512, as said below
- prompt_group: int32 [32], replicated, may hold values from 0 to 31, each once
Outputs:
- gated_out: bfloat16 [32, 4, 512, 2048], P('req', 'seq')
- final_states: float32 [32, 32, 64, 128], P(None, 'req', 'seq')
Inputs may be any that keep to these rules, and one draw needn't show every extreme that they name: Every prompt has 4 * lengths[p] tokens; some prompt has exactly 512 a device. Group prompt_group[p] holds prompt p; each group holds one prompt.
All inputs are finite; a program needn't handle non-finite values.
Results may differ from a plain program's by a relative error of at most 0.0059.
Values may be sent and summed in bfloat16 or wider, within the bound.
No kernel may reach another device: no remote copies, remote signals or barrier semaphores. Data moves between devices by JAX's collectives and lax.ppermute only.
A program may use at most 128 MiB of HBM per device.

v0:
```python
import jax
import jax.numpy as jnp
from jax import lax
from jax.sharding import PartitionSpec as P

BLOCK = 256


def shifted(block, axis, distance):
    devices = range(lax.axis_size(axis))
    route = [(i - distance, i) for i in devices if i - distance in devices]
    return lax.ppermute(block, axis, route)


def block_step(state, pieces):
    inputs_x, b_rows, c_rows, step_dt, log_decay = pieces
    length = inputs_x.shape[0]
    heads = step_dt.shape[1]
    hdim = inputs_x.shape[1] // heads
    running = jnp.cumsum(log_decay, axis=0)
    gram = jnp.einsum("tn,un->tu", c_rows, b_rows, preferred_element_type=jnp.float32)
    later = jnp.arange(length)[:, None] >= jnp.arange(length)[None, :]
    spread = running.T[:, :, None] - running.T[:, None, :]
    decay = jnp.where(later[None], jnp.exp(jnp.where(later[None], spread, 0.0)), 0.0)
    mixing = (gram[None] * decay * step_dt.T[:, None, :]).astype(jnp.bfloat16)
    heads_x = inputs_x.reshape(length, heads, hdim)
    inside = jnp.einsum("htu,uhp->thp", mixing, heads_x, preferred_element_type=jnp.float32)
    carried = jnp.exp(running)[:, :, None] * jnp.einsum(
        "tn,hpn->thp", c_rows.astype(jnp.float32), state, precision=lax.Precision.HIGHEST
    )
    final_log = running[-1]
    weighting = jnp.exp(final_log[None, :] - running) * step_dt
    weighted = (
        (heads_x.astype(jnp.float32) * weighting[:, :, None])
        .astype(jnp.bfloat16)
        .reshape(length, heads * hdim)
    )
    contrib = jnp.einsum("ud,un->dn", weighted, b_rows, preferred_element_type=jnp.float32).reshape(
        heads, hdim, -1
    )
    new_state = jnp.exp(final_log)[:, None, None] * state + contrib
    return (new_state, (inside + carried).reshape(length, heads * hdim))


def local(
    hidden, w_in, conv_weight, conv_bias, dt_bias, a_log, d_skip, norm_weight, lengths, prompt_group
):
    tok_rows = hidden[0, 0]
    slots = tok_rows.shape[0]
    inner = norm_weight.shape[0]
    heads = dt_bias.shape[0]
    hdim = inner // heads
    nstate = (conv_bias.shape[0] - inner) // 2
    convdim = conv_bias.shape[0]
    taps = conv_weight.shape[0]
    seq_count = lax.axis_size("seq")
    my_group = lax.axis_index("req")
    my_block = lax.axis_index("seq")
    qlen = jnp.sum(jnp.where(prompt_group == my_group, lengths, 0))
    filled = jnp.arange(slots, dtype=jnp.int32) < qlen
    wide_rows = lax.all_gather(w_in, "seq", axis=1, tiled=True)
    projected = jnp.dot(
        tok_rows,
        lax.all_gather(wide_rows, "req", axis=0, tiled=True),
        preferred_element_type=jnp.float32,
    ).astype(jnp.bfloat16)
    gate_z = projected[:, :inner]
    conv_in = projected[:, inner : inner + convdim]
    dt_raw = projected[:, inner + convdim :]
    edge_rows = lax.dynamic_slice_in_dim(conv_in, qlen - (taps - 1), taps - 1, 0)
    prev_edge = shifted(edge_rows, "seq", 1)
    extended = jnp.concatenate([prev_edge, conv_in], axis=0)
    accum = jnp.zeros((slots, convdim), jnp.float32) + conv_bias[None, :]
    for tap_index in range(taps):
        accum = accum + conv_weight[tap_index][None, :] * extended[
            tap_index : tap_index + slots
        ].astype(jnp.float32)
    conv_act = jax.nn.silu(accum).astype(jnp.bfloat16)
    inputs_x = conv_act[:, :inner]
    b_rows = conv_act[:, inner : inner + nstate]
    c_rows = conv_act[:, inner + nstate :]
    step_dt = jnp.where(
        filled[:, None], jax.nn.softplus(dt_raw.astype(jnp.float32) + dt_bias[None, :]), 0.0
    )
    log_decay = step_dt * (-jnp.exp(a_log))[None, :]
    through = jnp.cumsum(log_decay, axis=0)
    block_total = through[-1]
    block_rows = min(BLOCK, slots)
    count = slots // block_rows
    pieces = (
        inputs_x.reshape(count, block_rows, inner),
        b_rows.reshape(count, block_rows, nstate),
        c_rows.reshape(count, block_rows, nstate),
        step_dt.reshape(count, block_rows, heads),
        log_decay.reshape(count, block_rows, heads),
    )
    zero_state = jnp.zeros((heads, hdim, nstate), jnp.float32)
    local_end, outputs = lax.scan(block_step, zero_state, pieces)
    decays_all = lax.all_gather(block_total[None, :], "seq", axis=0, tiled=True)
    after_mine = jnp.sum(
        jnp.where(jnp.arange(seq_count)[:, None] > my_block, decays_all, 0.0), axis=0
    )
    entering = zero_state
    for turn in range(seq_count - 1):
        entering = shifted(jnp.exp(block_total)[:, None, None] * entering + local_end, "seq", 1)
    incoming = jnp.exp(through)[:, :, None] * jnp.einsum(
        "tn,hpn->thp", c_rows.astype(jnp.float32), entering, precision=lax.Precision.HIGHEST
    )
    heads_y = (
        outputs.reshape(slots, heads, hdim)
        + incoming
        + d_skip[None, :, None] * inputs_x.astype(jnp.float32).reshape(slots, heads, hdim)
    )
    gated = heads_y.reshape(slots, inner) * jax.nn.silu(gate_z.astype(jnp.float32))
    scale = lax.rsqrt(jnp.mean(gated * gated, axis=1, keepdims=True) + 1e-05)
    normed = jnp.where(filled[:, None], gated * scale * norm_weight[None, :], 0.0)
    gated_out = normed.astype(jnp.bfloat16).reshape(1, 1, slots, inner)
    decayed_end = jnp.exp(after_mine)[:, None, None] * local_end
    share = lax.psum_scatter(decayed_end, "seq", scatter_dimension=1, tiled=True)
    moved = lax.all_to_all(share[None], "req", split_axis=1, concat_axis=0, tiled=True)
    final_states = jnp.take(moved, prompt_group, axis=0)
    return (gated_out, final_states)


def solution(mesh):
    in_specs = (
        P("req", "seq", None, None),
        P("req", "seq"),
        P(),
        P(),
        P(),
        P(),
        P(),
        P(),
        P(),
        P(),
    )
    out_specs = (P("req", "seq", None, None), P(None, "req", "seq", None))
    return jax.shard_map(local, mesh=mesh, in_specs=in_specs, out_specs=out_specs, check_vma=False)
```

profile of v0, /device:TPU:7, one launch (start us, length us, event | category | flops | bytes accessed | tf_op | source)
XLA Modules:
  0.0 385.6 jit_solution(3540427270740208996)
XLA Ops:
  7.2 10.4 %all-gather = bf16[4,1096,64]{1,2,0:T(8,128)(2,1)S(1)} all-gather(bf16[1,1096,64]{1,2,0:T(8,128)(2,1)} %bitcast.173), channel_id=1, replica_groups=mesh['req'=32,'seq'=4] {'seq'}, dimensions={0}, use_global_device_ids=true | all-gather | bytes 701440 | tf_op jit(solution)/shard_map/all_gather | solution.py:61
  24.4 77.4 %all-gather.4.cloned.1.call-done = bf16[2048,4384]{1,0:T(8,128)(2,1)} async-done(((bf16[64,4384]{1,0:T(8,128)(2,1)}), bf16[2048,4384]{1,0:T(8,128)(2,1)}) %all-gather.4.cloned.1.call-update) | async-done | bytes 17956880 | tf_op jit(solution)/shard_map/all_gather | solution.py:64
  101.8 15.3 %convolution_convert_fusion = bf16[512,4384]{0,1:T(8,128)(2,1)} fusion(bf16[2048,4384]{1,0:T(8,128)(2,1)} %all-gather.4.cloned.1.call-done, bf16[1,1,512,2048]{3,2,1,0:T(8,128)(2,1)S(1)} %copy-done), kind=kOutput, calls=%fused_computation.45 | convolution fusion | flops 9196158976 | bytes 24543232 | tf_op jit(solution)/shard_map/dot_general | solution.py:62
  117.1 1.8 slice.81
  127.2 10.5 %multiply_convert_fusion.4 = bf16[512,2304]{0,1:T(8,128)(2,1)S(1)} fusion(bf16[512,2304]{0,1:T(8,128)(2,1)} %copy-done.5, bf16[3,2304]{0,1:T(8,128)(2,1)S(1)} %copy.57, f32[2304]{0:T(1024)S(1)} %get-tuple-element.118, f32[2304]{0:T(1024)S(1)} %get-tuple-element.119, f32[2304]{0:T(1024)S(1)} %get-tuple-element.117, f32[2304]{0:T(1024)S(1)} %get-tuple-element.116, ...), kind=kLoop, calls=%fused_computation.48 | loop fusion | flops 30670848 | bytes 4778496 | tf_op jit(solution)/shard_map/convert_element_type | solution.py:78
  138.6 1.8 copy.104
  141.6 117.3 %while.13 = (s32[]{:T(128)}, f32[32,64,128]{2,1,0:T(8,128)S(1)}, f32[2,256,2048]{1,0,2:T(2,128)}, f32[2,256,32]{1,0,2:T(2,128)S(1)}, bf16[2,256,2048]{1,2,0:T(8,...) while((s32[]{:T(128)}, f32[32,64,128]{2,1,0:T(8,128)S(1)}, ...), condition=%wide.region_4.5_spmd.clone, body=%wide.region_1.4_spmd.clone.sunk | while | flops 1242128512 | bytes 25203156 | solution.py:98
  147.0 2.7 bitcast_add_fusion.2
  149.7 8.6 %copy.117 = f32[1,256,2048]{1,0,2:T(1,128)S(1)} copy(f32[1,256,2048]{1,2,0:T(8,128)S(1)} %bitcast.161) | data formatting | bytes 4194304 | tf_op jit(solution)/shard_map/while/body/jit(dynamic_update_index_in_dim)/dynamic_update_slice | solution.py:98
  158.3 42.0 %dynamic_update_slice.6 = f32[2,256,2048]{1,0,2:T(2,128)} dynamic-update-slice(f32[2,256,2048]{1,0,2:T(2,128)} %get-tuple-element.231, f32[1,256,2048]{1,0,2:T(1,128)S(1)} %copy.117, s32[]{:T(128)S(6)} %copy.122, s32[]{:T(128)} %constant.60.clone.1..sunk, s32[]{:T(128)} %constant.60.clone.1..sunk) | dynamic-update-slice | bytes 4194308 | tf_op jit(solution)/shard_map/while/body/jit(dynamic_update_index_in_dim)/dynamic_update_slice | solution.py:98
  205.7 2.7 bitcast_add_fusion.2
  208.4 8.6 %copy.117 = f32[1,256,2048]{1,0,2:T(1,128)S(1)} copy(f32[1,256,2048]{1,2,0:T(8,128)S(1)} %bitcast.161) | data formatting | bytes 4194304 | tf_op jit(solution)/shard_map/while/body/jit(dynamic_update_index_in_dim)/dynamic_update_slice | solution.py:98
  216.9 42.0 %dynamic_update_slice.6 = f32[2,256,2048]{1,0,2:T(2,128)} dynamic-update-slice(f32[2,256,2048]{1,0,2:T(2,128)} %get-tuple-element.231, f32[1,256,2048]{1,0,2:T(1,128)S(1)} %copy.117, s32[]{:T(128)S(6)} %copy.122, s32[]{:T(128)} %constant.60.clone.1..sunk, s32[]{:T(128)} %constant.60.clone.1..sunk) | dynamic-update-slice | bytes 4194308 | tf_op jit(solution)/shard_map/while/body/jit(dynamic_update_index_in_dim)/dynamic_update_slice | solution.py:98
  261.1 27.8 %all-gather.1 = f32[4,1,32]{2,1,0:T(1,128)S(1)} all-gather(f32[1,1,32]{2,1,0:T(1,128)} %bitcast.175), channel_id=1, replica_groups=mesh['req'=32,'seq'=4] {'seq'}, dimensions={0}, use_global_device_ids=true | all-gather | bytes 640 | tf_op jit(solution)/shard_map/all_gather | solution.py:99
  291.5 22.9 %collective-permute-done.2 = f32[32,64,128]{2,1,0:T(8,128)S(1)} collective-permute-done((f32[32,64,128]{2,1,0:T(8,128)S(1)}, f32[32,64,128]{2,1,0:T(8,128)S(1)}, u32[]{:S(2)}, u32[]{:S(2)}) %collective-permute-start.2) | collective-permute-done | bytes 1048608 | tf_op jit(solution)/shard_map/ppermute | solution.py:12
  317.3 6.4 %reshape.162 = f32[512,32,64]{0,2,1:T(8,128)} reshape(f32[2,256,2048]{1,0,2:T(2,128)} %get-tuple-element.45) | data formatting | bytes 8388608 | tf_op jit(solution)/shard_map/reshape | solution.py:110
  323.7 23.2 %collective-permute-done.3 = f32[32,64,128]{2,1,0:T(8,128)S(1)} collective-permute-done((f32[32,64,128]{2,1,0:T(8,128)}, f32[32,64,128]{2,1,0:T(8,128)S(1)}, u32[]{:S(2)}, u32[]{:S(2)}) %collective-permute-start.3) | collective-permute-done | bytes 1048608 | tf_op jit(solution)/shard_map/ppermute | solution.py:12
  347.0 2.7 fusion.37
  349.7 3.8 fusion.31
  353.5 1.9 copy-done.2
  355.4 3.0 multiply_reduce_fusion
  358.5 9.9 %all-to-all-start = ((f32[1,32,16,128]{3,2,0,1:T(8,128)}), f32[1,32,16,128]{3,2,0,1:T(8,128)S(1)}, u32[]{:S(2)}, u32[]{:S(2)}) async-start(f32[1,32,16,128]{3,2,0,1:T(8,128)} %bitcast.171), calls=%async_computation.1 | async-start | bytes 524288 | tf_op jit(solution)/shard_map/all_to_all | solution.py:120
  368.5 4.8 %fusion.34 = bf16[1,1,512,2048]{2,3,1,0:T(8,128)(2,1)} fusion(f32[2048]{0:T(1024)S(1)} %copy-done.12, f32[512]{0:T(512)S(1)} %add_rsqrt_fusion, pred[512]{0:T(512)(128)(4,1)S(1)} %iota_compare_fusion.1, bf16[512,4384]{0,1:T(8,128)(2,1)} %convolution_convert_fusion, f32[512,32,64]{0,2,1:T(8,128)} %copy-done.2), kind=kLoop, calls=%fused_computation.64 | loop fusion | flops 10485760 | bytes 8399360 | tf_op jit(solution)/shard_map/reshape | solution.py:117
  373.3 3.9 %copy.67 = bf16[1,1,512,2048]{3,2,1,0:T(8,128)(2,1)} copy(bf16[1,1,512,2048]{2,3,1,0:T(8,128)(2,1)} %fusion.34) | data formatting | bytes 4194304
  (117 shorter events, 35.4 us)
Async XLA Ops:
  7.2 94.6 %copy-start = (bf16[1,1,512,2048]{3,2,1,0:T(8,128)(2,1)S(1)}, bf16[1,1,512,2048]{3,2,1,0:T(8,128)(2,1)}, u32[]{:S(2)}) copy-start(bf16[1,1,512,2048]{3,2,1,0:T(8,128)(2,1)} %param.12) | copy-start | bytes 6291460
  7.2 94.6 %all-gather.4.cloned.1.call-start = ((), (), s32[]{:S(2)}) async-start(), calls=%async_computation.2 | async-start | bytes 18923520 | tf_op jit(solution)/shard_map/all_gather | solution.py:64
  19.3 339.2 %reduce-scatter.2.cloned.1.call-start = ((), (), s32[]{:S(2)}) async-start(), calls=%async_computation.3 | async-start | bytes 1310720 | tf_op jit(solution)/shard_map/reduce_scatter | solution.py:119
  117.1 5.3 %copy-start.13 = (f32[32]{0:T(128)S(1)}, f32[32]{0:T(128)}, u32[]{:S(2)}) copy-start(f32[32]{0:T(128)} %param.16) | copy-start | bytes 388
  117.1 10.0 %copy-start.11 = (f32[2304]{0:T(1024)S(1)}, f32[2304]{0:T(1024)}, u32[]{:S(2)}) copy-start(f32[2304]{0:T(1024)} %param.15) | copy-start | bytes 27652
  120.9 5.9 %collective-permute-start = (bf16[3,2304]{1,0:T(4,128)(2,1)S(1)}, bf16[3,2304]{1,0:T(4,128)(2,1)S(1)}, u32[]{:S(2)}, u32[]{:S(2)}) collective-permute-start(bf16[3,2304]{1,0:T(4,128)(2,1)S(1)} %copy.56), channel_id=1, source_target_pairs={{0,1},{1,2},{2,3},{4,5},{5,6},{6,7},{8,9},{9,10},{10,11},{12,13},{... | collective-permute-start | bytes 41480 | tf_op jit(solution)/shard_map/ppermute | solution.py:12
  124.4 2.4 copy-start.7
  137.6 2.9 copy-start.6
  137.8 3.9 %copy-start.3 = (bf16[512,2048]{0,1:T(8,128)(2,1)}, bf16[512,2048]{0,1:T(8,128)(2,1)S(1)}, u32[]{:S(2)}) copy-start(bf16[512,2048]{0,1:T(8,128)(2,1)S(1)} %slice.86) | copy-start | bytes 6291460
  141.6 1.9 copy-start.9
  149.7 50.6 %copy-start.10 = (f32[2,256,32]{1,0,2:T(2,128)S(1)}, f32[2,256,32]{1,0,2:T(2,128)}, u32[]{:S(2)}) copy-start(f32[2,256,32]{1,0,2:T(2,128)} %copy-done.9) | copy-start | bytes 196612 | tf_op jit(solution)/shard_map/while
  200.3 1.9 copy-start.9
  208.4 50.6 %copy-start.10 = (f32[2,256,32]{1,0,2:T(2,128)S(1)}, f32[2,256,32]{1,0,2:T(2,128)}, u32[]{:S(2)}) copy-start(f32[2,256,32]{1,0,2:T(2,128)} %copy-done.9) | copy-start | bytes 196612 | tf_op jit(solution)/shard_map/while
  259.8 57.4 %copy-start.15 = (s32[32]{0:T(128)S(1)}, s32[32]{0:T(128)}, u32[]{:S(2)}) copy-start(s32[32]{0:T(128)} %param.21) | copy-start | bytes 388
  259.8 29.2 %collective-permute-start.1 = (f32[32,64,128]{2,1,0:T(8,128)S(1)}, f32[32,64,128]{2,1,0:T(8,128)S(1)}, u32[]{:S(2)}, u32[]{:S(2)}) collective-permute-start(f32[32,64,128]{2,1,0:T(8,128)S(1)} %broadcast_add_fusion), channel_id=1, source_target_pairs={{0,1},{1,2},{2,3},{4,5},{5,6},{6,7},{8,9},{9,10},{10,11},{12,13},{... | collective-permute-start | bytes 3145736 | tf_op jit(solution)/shard_map/ppermute | solution.py:12
  289.0 28.2 %copy-start.8 = (f32[32,4,128]{2,0,1:T(8,128)S(1)}, f32[32,4,128]{2,0,1:T(8,128)}, u32[]{:S(2)}) copy-start(f32[32,4,128]{2,0,1:T(8,128)} %copy-done.7) | copy-start | bytes 196612
  290.2 24.2 %collective-permute-start.2 = (f32[32,64,128]{2,1,0:T(8,128)S(1)}, f32[32,64,128]{2,1,0:T(8,128)S(1)}, u32[]{:S(2)}, u32[]{:S(2)}) collective-permute-start(f32[32,64,128]{2,1,0:T(8,128)S(1)} %get-tuple-element.150), channel_id=1, source_target_pairs={{0,1},{1,2},{2,3},{4,5},{5,6},{6,7},{8,9},{9,10},{10,11},{12,13},{... | collective-permute-start | bytes 3145736 | tf_op jit(solution)/shard_map/ppermute | solution.py:12
  315.6 31.3 %collective-permute-start.3 = (f32[32,64,128]{2,1,0:T(8,128)}, f32[32,64,128]{2,1,0:T(8,128)S(1)}, u32[]{:S(2)}, u32[]{:S(2)}) collective-permute-start(f32[32,64,128]{2,1,0:T(8,128)} %multiply_add_fusion), channel_id=1, source_target_pairs={{0,1},{1,2},{2,3},{4,5},{5,6},{6,7},{8,9},{9,10},{10,11},{12,13},{... | collective-permute-start | bytes 3145736 | tf_op jit(solution)/shard_map/ppermute | solution.py:12
  323.7 25.9 %copy-start.4 = (bf16[512,2048]{0,1:T(8,128)(2,1)S(1)}, bf16[512,2048]{0,1:T(8,128)(2,1)}, u32[]{:S(2)}) copy-start(bf16[512,2048]{0,1:T(8,128)(2,1)} %copy-done.3) | copy-start | bytes 6291460
  323.7 25.9 %copy-start.14 = (f32[32]{0:T(128)S(1)}, f32[32]{0:T(128)}, u32[]{:S(2)}) copy-start(f32[32]{0:T(128)} %param.18) | copy-start | bytes 388
  353.5 1.9 copy-start.2
  355.4 13.0 %copy-start.12 = (f32[2048]{0:T(1024)S(1)}, f32[2048]{0:T(1024)}, u32[]{:S(2)}) copy-start(f32[2048]{0:T(1024)} %param.19) | copy-start | bytes 24580
  358.5 18.8 %all-to-all-start = ((f32[1,32,16,128]{3,2,0,1:T(8,128)}), f32[1,32,16,128]{3,2,0,1:T(8,128)S(1)}, u32[]{:S(2)}, u32[]{:S(2)}) async-start(f32[1,32,16,128]{3,2,0,1:T(8,128)} %bitcast.171), calls=%async_computation.1 | async-start | bytes 524288 | tf_op jit(solution)/shard_map/all_to_all | solution.py:120
  368.5 10.3 %copy-start.1 = (bf16[1,1,512,2048]{3,2,1,0:T(8,128)(2,1)S(1)}, bf16[1,1,512,2048]{3,2,1,0:T(8,128)(2,1)}, u32[]{:S(2)}) copy-start(bf16[1,1,512,2048]{3,2,1,0:T(8,128)(2,1)} %param.12) | copy-start | bytes 6291460
  (1 other events, 1.4 us)
Sparse Core Ops, SparseCore 0:
  19.4 82.3 all-gather.3
  317.3 31.4 reduce-scatter.1
where the time goes:
time: 392 us; the launch traced here: 386 us
  local copies, waits for them, and re-layouts  129 us (33%)
  waiting for transfers between devices  124 us (32%)
  blocking collectives  38.1 us (10%)
  other arithmetic  36.4 us (9%)
  matrix products  26.7 us (7%)
  between operations  15.7 us (4%)
  starting transfers between devices  15.5 us (4%)
    dynamic_update_slice x4, local copies, waits for them, and re-layouts, local(): local_end, outputs = lax.scan(block_step, zero_state, pieces)  101 us
    all_gather x1, waiting for transfers between devices, local(): lax.all_gather(wide_rows, 'req', axis=0, tiled=True)  77.4 us
    ppermute x4, waiting for transfers between devices, shifted(): return lax.ppermute(block, axis, route)  46.2 us
    all_gather x1, blocking collectives, local(): decays_all = lax.all_gather(block_total[None, :], 'seq', axis=0, tiled=True)  27.8 us
    dot_general x1, matrix products, local(): jnp.dot(tok_rows, lax.all_gather(wide_rows, 'req', axis=0, tiled=True), p...  15.3 us
    convert_element_type x1, other arithmetic, local(): conv_act = jax.nn.silu(accum).astype(jnp.bfloat16)  10.5 us
    all_gather x1, blocking collectives, local(): wide_rows = lax.all_gather(w_in, 'seq', axis=1, tiled=True)  10.4 us
    all_to_all x1, starting transfers between devices, local(): lax.all_to_all(share[None], 'req', split_axis=1, concat_axis=0, tiled=True)  9.92 us
  transfers between devices with their start and end apart: 7, of which 4 were waited for; matrix products, arithmetic and copies ran while one was open for 9% of the time, Pallas kernels for 0%

commit v1 on v0

--- a/solution.py
+++ b/solution.py
@@ -58,7 +58,12 @@
     my_block = lax.axis_index("seq")
     qlen = jnp.sum(jnp.where(prompt_group == my_group, lengths, 0))
     filled = jnp.arange(slots, dtype=jnp.int32) < qlen
-    wide_rows = lax.all_gather(w_in, "seq", axis=1, tiled=True)
+    ring = [w_in]
+    for hop in range(3):
+        ring.append(lax.ppermute(ring[-1], "seq", [(dev, (dev + 1) % 4) for dev in range(4)]))
+    wide_rows = jnp.roll(
+        jnp.concatenate(ring[::-1], axis=1), (lax.axis_index("seq") + 1) * ring[0].shape[1], axis=1
+    )
     projected = jnp.dot(
         tok_rows,
         lax.all_gather(wide_rows, "req", axis=0, tiled=True),

time: 392 us -> 397 us (1.013)
  waiting for transfers between devices: 124 us -> 135 us
  blocking collectives: 38.1 us -> 27.8 us
    all_gather x1 -> x0, blocking collectives: 10.4 us -> none  [local(): wide_rows = lax.all_gather(w_in, 'seq', axis=1, tiled=True)]
    ppermute x0 -> x3, waiting for transfers between devices: none -> 9.92 us  [local(): lax.ppermute(ring[-1], 'seq', [(dev, (dev + 1) % 4) for dev in range(4)])]
    unnamed x32 -> x33, local copies, waits for them, and re-layouts: 9.68 us -> 10.6 us
  transfers between devices with their start and end apart: 7 -> 10, of which waited for: 4 -> 7; matrix products, arithmetic and copies ran while one was open for 9% -> 8% of each run, Pallas kernels for 0% -> 0%
where the time goes in v1:
time: 397 us; the launch traced here: 390 us
  waiting for transfers between devices  135 us (34%)
  local copies, waits for them, and re-layouts  131 us (33%)
  other arithmetic  36.4 us (9%)
  blocking collectives  27.8 us (7%)
  matrix products  25.4 us (6%)
  starting transfers between devices  18.9 us (5%)
  between operations  15.7 us (4%)
    dynamic_update_slice x4, local copies, waits for them, and re-layouts, local(): local_end, outputs = lax.scan(block_step, zero_state, pieces)  101 us
    all_gather x1, waiting for transfers between devices, local(): lax.all_gather(wide_rows, 'req', axis=0, tiled=True)  78.2 us
    ppermute x4, waiting for transfers between devices, shifted(): return lax.ppermute(block, axis, route)  46.2 us
    all_gather x1, blocking collectives, local(): decays_all = lax.all_gather(block_total[None, :], 'seq', axis=0, tiled=True)  27.8 us
    dot_general x1, matrix products, local(): jnp.dot(tok_rows, lax.all_gather(wide_rows, 'req', axis=0, tiled=True), p...  14 us
    unnamed x33, local copies, waits for them, and re-layouts  10.6 us
    convert_element_type x1, other arithmetic, local(): conv_act = jax.nn.silu(accum).astype(jnp.bfloat16)  10.6 us
    ppermute x3, waiting for transfers between devices, local(): lax.ppermute(ring[-1], 'seq', [(dev, (dev + 1) % 4) for dev in range(4)])  9.92 us
  transfers between devices with their start and end apart: 10, of which 7 were waited for; matrix products, arithmetic and copies ran while one was open for 8% of the time, Pallas kernels for 0%

profile of v1, /device:TPU:7, one launch (start us, length us, event | category | flops | bytes accessed | tf_op | source)
XLA Modules:
  0.0 390.5 jit_solution(17807515857828950228)
XLA Ops:
  7.3 4.9 %collective-permute-done = bf16[64,1096]{1,0:T(8,128)(2,1)S(1)} collective-permute-done((bf16[64,1096]{1,0:T(8,128)(2,1)}, bf16[64,1096]{1,0:T(8,128)(2,1)S(1)}, u32[]{:S(2)}, u32[]{:S(2)}) %collective-permute-start) | collective-permute-done | bytes 140320 | tf_op jit(solution)/shard_map/ppermute | solution.py:63
  13.3 2.9 collective-permute-done.1
  16.2 2.3 collective-permute-start.2
  20.6 2.6 concatenate.9
  29.3 78.2 %all-gather.3.cloned.1.call-done = bf16[2048,4384]{1,0:T(8,128)(2,1)} async-done(((bf16[64,4384]{1,0:T(8,128)(2,1)}), bf16[2048,4384]{1,0:T(8,128)(2,1)}) %all-gather.3.cloned.1.call-update) | async-done | bytes 17956880 | tf_op jit(solution)/shard_map/all_gather | solution.py:69
  107.5 14.0 %fusion.27 = bf16[512,4384]{0,1:T(8,128)(2,1)S(1)} fusion(bf16[2048,4384]{1,0:T(8,128)(2,1)} %all-gather.3.cloned.1.call-done, bf16[1,1,512,2048]{3,2,1,0:T(8,128)(2,1)S(1)} %copy-done), kind=kOutput, calls=%fused_computation.46 | convolution fusion | flops 9196158976 | bytes 24543232 | tf_op jit(solution)/shard_map/dot_general | solution.py:67
  132.0 10.6 %multiply_convert_fusion.4 = bf16[512,2304]{0,1:T(8,128)(2,1)S(1)} fusion(bf16[512,2304]{0,1:T(8,128)(2,1)} %copy-done.5, bf16[3,2304]{0,1:T(8,128)(2,1)S(1)} %copy.54, f32[2304]{0:T(1024)S(1)} %get-tuple-element.118, f32[2304]{0:T(1024)S(1)} %get-tuple-element.119, f32[2304]{0:T(1024)S(1)} %get-tuple-element.117, f32[2304]{0:T(1024)S(1)} %get-tuple-element.116, ...), kind=kLoop, calls=%fused_computation.49 | loop fusion | flops 30670848 | bytes 4778496 | tf_op jit(solution)/shard_map/convert_element_type | solution.py:83
  146.5 117.3 %while.13 = (s32[]{:T(128)}, f32[32,64,128]{2,1,0:T(8,128)S(1)}, f32[2,256,2048]{1,0,2:T(2,128)}, f32[2,256,32]{1,0,2:T(2,128)S(1)}, bf16[2,256,2048]{1,2,0:T(8,...) while((s32[]{:T(128)}, f32[32,64,128]{2,1,0:T(8,128)S(1)}, ...), condition=%wide.region_4.5_spmd.clone, body=%wide.region_1.4_spmd.clone.sunk | while | flops 1242128512 | bytes 25203156 | solution.py:103
  151.9 2.7 bitcast_add_fusion.2
  154.6 8.6 %copy.114 = f32[1,256,2048]{1,0,2:T(1,128)S(1)} copy(f32[1,256,2048]{1,2,0:T(8,128)S(1)} %bitcast.157) | data formatting | bytes 4194304 | tf_op jit(solution)/shard_map/while/body/jit(dynamic_update_index_in_dim)/dynamic_update_slice | solution.py:103
  163.2 42.0 %dynamic_update_slice.6 = f32[2,256,2048]{1,0,2:T(2,128)} dynamic-update-slice(f32[2,256,2048]{1,0,2:T(2,128)} %get-tuple-element.231, f32[1,256,2048]{1,0,2:T(1,128)S(1)} %copy.114, s32[]{:T(128)S(6)} %copy.119, s32[]{:T(128)} %constant.78.clone.1..sunk, s32[]{:T(128)} %constant.78.clone.1..sunk) | dynamic-update-slice | bytes 4194308 | tf_op jit(solution)/shard_map/while/body/jit(dynamic_update_index_in_dim)/dynamic_update_slice | solution.py:103
  210.6 2.7 bitcast_add_fusion.2
  213.3 8.6 %copy.114 = f32[1,256,2048]{1,0,2:T(1,128)S(1)} copy(f32[1,256,2048]{1,2,0:T(8,128)S(1)} %bitcast.157) | data formatting | bytes 4194304 | tf_op jit(solution)/shard_map/while/body/jit(dynamic_update_index_in_dim)/dynamic_update_slice | solution.py:103
  221.9 42.0 %dynamic_update_slice.6 = f32[2,256,2048]{1,0,2:T(2,128)} dynamic-update-slice(f32[2,256,2048]{1,0,2:T(2,128)} %get-tuple-element.231, f32[1,256,2048]{1,0,2:T(1,128)S(1)} %copy.114, s32[]{:T(128)S(6)} %copy.119, s32[]{:T(128)} %constant.78.clone.1..sunk, s32[]{:T(128)} %constant.78.clone.1..sunk) | dynamic-update-slice | bytes 4194308 | tf_op jit(solution)/shard_map/while/body/jit(dynamic_update_index_in_dim)/dynamic_update_slice | solution.py:103
  266.0 27.8 %all-gather = f32[4,1,32]{2,1,0:T(1,128)S(1)} all-gather(f32[1,1,32]{2,1,0:T(1,128)} %bitcast.169), channel_id=1, replica_groups=mesh['req'=32,'seq'=4] {'seq'}, dimensions={0}, use_global_device_ids=true | all-gather | bytes 640 | tf_op jit(solution)/shard_map/all_gather | solution.py:104
  296.4 22.9 %collective-permute-done.5 = f32[32,64,128]{2,1,0:T(8,128)S(1)} collective-permute-done((f32[32,64,128]{2,1,0:T(8,128)S(1)}, f32[32,64,128]{2,1,0:T(8,128)S(1)}, u32[]{:S(2)}, u32[]{:S(2)}) %collective-permute-start.5) | collective-permute-done | bytes 1048608 | tf_op jit(solution)/shard_map/ppermute | solution.py:12
  322.1 6.5 %reshape.162 = f32[512,32,64]{0,2,1:T(8,128)} reshape(f32[2,256,2048]{1,0,2:T(2,128)} %get-tuple-element.45) | data formatting | bytes 8388608 | tf_op jit(solution)/shard_map/reshape | solution.py:115
  328.6 23.2 %collective-permute-done.6 = f32[32,64,128]{2,1,0:T(8,128)S(1)} collective-permute-done((f32[32,64,128]{2,1,0:T(8,128)}, f32[32,64,128]{2,1,0:T(8,128)S(1)}, u32[]{:S(2)}, u32[]{:S(2)}) %collective-permute-start.6) | collective-permute-done | bytes 1048608 | tf_op jit(solution)/shard_map/ppermute | solution.py:12
  351.9 2.7 fusion.38
  354.6 3.8 fusion.32
  360.4 3.0 multiply_reduce_fusion
  363.5 9.9 %all-to-all-start = ((f32[1,32,16,128]{3,2,0,1:T(8,128)}), f32[1,32,16,128]{3,2,0,1:T(8,128)S(1)}, u32[]{:S(2)}, u32[]{:S(2)}) async-start(f32[1,32,16,128]{3,2,0,1:T(8,128)} %bitcast.166), calls=%async_computation.1 | async-start | bytes 524288 | tf_op jit(solution)/shard_map/all_to_all | solution.py:125
  373.4 4.8 %fusion.35 = bf16[1,1,512,2048]{2,3,1,0:T(8,128)(2,1)} fusion(f32[2048]{0:T(1024)S(1)} %copy-done.13, f32[512]{0:T(512)S(1)} %add_rsqrt_fusion, pred[512]{0:T(512)(128)(4,1)S(1)} %iota_compare_fusion.1, bf16[512,4384]{0,1:T(8,128)(2,1)} %copy-done.7, f32[512,32,64]{0,2,1:T(8,128)} %copy-done.2), kind=kLoop, calls=%fused_computation.65 | loop fusion | flops 10485760 | bytes 8399360 | tf_op jit(solution)/shard_map/reshape | solution.py:122
  378.1 3.9 %copy.64 = bf16[1,1,512,2048]{3,2,1,0:T(8,128)(2,1)} copy(bf16[1,1,512,2048]{2,3,1,0:T(8,128)(2,1)} %fusion.35) | data formatting | bytes 4194304
  (124 shorter events, 44.0 us)
Async XLA Ops:
  7.2 100.4 %copy-start = (bf16[1,1,512,2048]{3,2,1,0:T(8,128)(2,1)S(1)}, bf16[1,1,512,2048]{3,2,1,0:T(8,128)(2,1)}, u32[]{:S(2)}) copy-start(bf16[1,1,512,2048]{3,2,1,0:T(8,128)(2,1)} %param.12) | copy-start | bytes 6291460
  7.2 100.3 %all-gather.3.cloned.1.call-start = ((), (), s32[]{:S(2)}) async-start(), calls=%async_computation.2 | async-start | bytes 18923520 | tf_op jit(solution)/shard_map/all_gather | solution.py:69
  7.2 5.0 %collective-permute-start = (bf16[64,1096]{1,0:T(8,128)(2,1)}, bf16[64,1096]{1,0:T(8,128)(2,1)S(1)}, u32[]{:S(2)}, u32[]{:S(2)}) collective-permute-start(bf16[64,1096]{1,0:T(8,128)(2,1)} %param.13), channel_id=1, source_target_pairs={{0,1},{1,2},{2,3},{3,0},{4,5},{5,6},{6,7},{7,4},{8,9},{9,10},{10,1... | collective-permute-start | bytes 420872 | tf_op jit(solution)/shard_map/ppermute | solution.py:63
  12.2 4.0 %collective-permute-start.1 = (bf16[64,1096]{1,0:T(8,128)(2,1)S(1)}, bf16[64,1096]{1,0:T(8,128)(2,1)S(1)}, u32[]{:S(2)}, u32[]{:S(2)}) collective-permute-start(bf16[64,1096]{1,0:T(8,128)(2,1)S(1)} %collective-permute-done), channel_id=1, source_target_pairs={{0,1},{1,2},{2,3},{3,0},{4,5},{5,6},{6,7},{7,4},{8,9},{9,10},{10,1... | collective-permute-start | bytes 420872 | tf_op jit(solution)/shard_map/ppermute | solution.py:63
  16.2 4.4 %collective-permute-start.2 = (bf16[64,1096]{1,0:T(8,128)(2,1)S(1)}, bf16[64,1096]{1,0:T(8,128)(2,1)}, u32[]{:S(2)}, u32[]{:S(2)}) collective-permute-start(bf16[64,1096]{1,0:T(8,128)(2,1)S(1)} %collective-permute-done.1), channel_id=1, source_target_pairs={{0,1},{1,2},{2,3},{3,0},{4,5},{5,6},{6,7},{7,4},{8,9},{9,10},{10,1... | collective-permute-start | bytes 420872 | tf_op jit(solution)/shard_map/ppermute | solution.py:63
  24.3 339.2 %reduce-scatter.2.cloned.1.call-start = ((), (), s32[]{:S(2)}) async-start(), calls=%async_computation.3 | async-start | bytes 1310720 | tf_op jit(solution)/shard_map/reduce_scatter | solution.py:124
  123.6 3.6 copy-start.14
  123.6 8.4 %copy-start.12 = (f32[2304]{0:T(1024)S(1)}, f32[2304]{0:T(1024)}, u32[]{:S(2)}) copy-start(f32[2304]{0:T(1024)} %param.15) | copy-start | bytes 27652
  125.7 5.9 %collective-permute-start.3 = (bf16[3,2304]{1,0:T(4,128)(2,1)S(1)}, bf16[3,2304]{1,0:T(4,128)(2,1)S(1)}, u32[]{:S(2)}, u32[]{:S(2)}) collective-permute-start(bf16[3,2304]{1,0:T(4,128)(2,1)S(1)} %copy.53), channel_id=1, source_target_pairs={{0,1},{1,2},{2,3},{4,5},{5,6},{6,7},{8,9},{9,10},{10,11},{12,13},{... | collective-permute-start | bytes 41480 | tf_op jit(solution)/shard_map/ppermute | solution.py:12
  129.3 2.3 copy-start.8
  142.5 2.9 copy-start.6
  142.7 3.9 copy-start.3
  154.6 50.6 %copy-start.11 = (f32[2,256,32]{1,0,2:T(2,128)S(1)}, f32[2,256,32]{1,0,2:T(2,128)}, u32[]{:S(2)}) copy-start(f32[2,256,32]{1,0,2:T(2,128)} %copy-done.10) | copy-start | bytes 196612 | tf_op jit(solution)/shard_map/while
  213.3 50.6 %copy-start.11 = (f32[2,256,32]{1,0,2:T(2,128)S(1)}, f32[2,256,32]{1,0,2:T(2,128)}, u32[]{:S(2)}) copy-start(f32[2,256,32]{1,0,2:T(2,128)} %copy-done.10) | copy-start | bytes 196612 | tf_op jit(solution)/shard_map/while
  264.7 57.3 %copy-start.16 = (s32[32]{0:T(128)S(1)}, s32[32]{0:T(128)}, u32[]{:S(2)}) copy-start(s32[32]{0:T(128)} %param.21) | copy-start | bytes 388
  264.7 29.2 %collective-permute-start.4 = (f32[32,64,128]{2,1,0:T(8,128)S(1)}, f32[32,64,128]{2,1,0:T(8,128)S(1)}, u32[]{:S(2)}, u32[]{:S(2)}) collective-permute-start(f32[32,64,128]{2,1,0:T(8,128)S(1)} %broadcast_add_fusion), channel_id=1, source_target_pairs={{0,1},{1,2},{2,3},{4,5},{5,6},{6,7},{8,9},{9,10},{10,11},{12,13},{... | collective-permute-start | bytes 3145736 | tf_op jit(solution)/shard_map/ppermute | solution.py:12
  293.9 28.2 %copy-start.9 = (f32[32,4,128]{2,0,1:T(8,128)S(1)}, f32[32,4,128]{2,0,1:T(8,128)}, u32[]{:S(2)}) copy-start(f32[32,4,128]{2,0,1:T(8,128)} %copy-done.8) | copy-start | bytes 196612
  295.1 24.2 %collective-permute-start.5 = (f32[32,64,128]{2,1,0:T(8,128)S(1)}, f32[32,64,128]{2,1,0:T(8,128)S(1)}, u32[]{:S(2)}, u32[]{:S(2)}) collective-permute-start(f32[32,64,128]{2,1,0:T(8,128)S(1)} %get-tuple-element.150), channel_id=1, source_target_pairs={{0,1},{1,2},{2,3},{4,5},{5,6},{6,7},{8,9},{9,10},{10,11},{12,13},{... | collective-permute-start | bytes 3145736 | tf_op jit(solution)/shard_map/ppermute | solution.py:12
  320.5 31.4 %collective-permute-start.6 = (f32[32,64,128]{2,1,0:T(8,128)}, f32[32,64,128]{2,1,0:T(8,128)S(1)}, u32[]{:S(2)}, u32[]{:S(2)}) collective-permute-start(f32[32,64,128]{2,1,0:T(8,128)} %multiply_add_fusion), channel_id=1, source_target_pairs={{0,1},{1,2},{2,3},{4,5},{5,6},{6,7},{8,9},{9,10},{10,11},{12,13},{... | collective-permute-start | bytes 3145736 | tf_op jit(solution)/shard_map/ppermute | solution.py:12
  328.6 25.9 %copy-start.4 = (bf16[512,2048]{0,1:T(8,128)(2,1)S(1)}, bf16[512,2048]{0,1:T(8,128)(2,1)}, u32[]{:S(2)}) copy-start(bf16[512,2048]{0,1:T(8,128)(2,1)} %copy-done.3) | copy-start | bytes 6291460
  328.6 25.9 %copy-start.15 = (f32[32]{0:T(128)S(1)}, f32[32]{0:T(128)}, u32[]{:S(2)}) copy-start(f32[32]{0:T(128)} %param.18) | copy-start | bytes 388
  360.4 12.9 %copy-start.13 = (f32[2048]{0:T(1024)S(1)}, f32[2048]{0:T(1024)}, u32[]{:S(2)}) copy-start(f32[2048]{0:T(1024)} %param.19) | copy-start | bytes 24580
  363.5 18.8 %all-to-all-start = ((f32[1,32,16,128]{3,2,0,1:T(8,128)}), f32[1,32,16,128]{3,2,0,1:T(8,128)S(1)}, u32[]{:S(2)}, u32[]{:S(2)}) async-start(f32[1,32,16,128]{3,2,0,1:T(8,128)} %bitcast.166), calls=%async_computation.1 | async-start | bytes 524288 | tf_op jit(solution)/shard_map/all_to_all | solution.py:125
  373.3 10.3 %copy-start.1 = (bf16[1,1,512,2048]{3,2,1,0:T(8,128)(2,1)S(1)}, bf16[1,1,512,2048]{3,2,1,0:T(8,128)(2,1)}, u32[]{:S(2)}) copy-start(bf16[1,1,512,2048]{3,2,1,0:T(8,128)(2,1)} %param.12) | copy-start | bytes 6291460
  (5 other events, 9.4 us)
Sparse Core Ops, SparseCore 0:
  24.4 83.0 all-gather.2
  322.2 31.4 reduce-scatter.1
